TPU v7x, 512 devices: a whole 4x8x8 slice. The times are simulated.
512 devices in a mesh: segment: 4 (over z_lo), seq: 16 (over z_hi, x, core), mp: 8 (over y).
Axes of the slice: x: 4, y: 8, z: 8 (z_hi: 2, z_lo: 4; z = z_hi * 4 + z_lo), core: 2. Of those that a mesh axis runs over, the one named last changes fastest.
Arguments:
- latents: bfloat16 [4, 16, 256, 4096], P('segment', 'seq', None, 'mp'), may hold values from -6 to 6
- w_qkv: bfloat16 [4, 4096, 3, 4096], P('segment', 'seq', None, 'mp'), may hold values from -1 to 1
- w_out: bfloat16 [4, 4096, 4096], P('segment', 'mp', 'seq'), may hold values from -0.09375 to 0.09375
- mod_shift: float32 [4, 4096], P('segment'), may hold values from -3 to 3
- mod_scale: float32 [4, 4096], P('segment'), may hold values from 0.1 to 1.9
- mod_gate: float32 [4, 4096], P('segment'), may hold values from 0.5 to 1.5
- counts: int32 [4, 16], P('segment'), may hold values from 64 to 256, as said below
Outputs:
- next_latents: bfloat16 [4, 16, 256, 4096], P('segment', 'seq', None, 'mp')
Inputs may be any that keep to these rules, and one draw needn't show every extreme that they name: `counts`: in every section's clip at least one frame has all 256 patch positions valid.
All inputs are finite; a program needn't handle non-finite values.
Results may differ from a plain program's by a relative error of at most 0.01.
Values may be sent and summed in bfloat16 or wider, within the bound.
No kernel may reach another device: no remote copies, remote signals or barrier semaphores. Data moves between devices by JAX's collectives and lax.ppermute only.
A program may use at most 64 MiB of HBM per device.

v0:
```python
import math
import jax
import jax.numpy as jnp
from jax import lax
from jax.sharding import PartitionSpec as P

HD = 128
EPS = 1e-06
NEG_FILL = -1e30


def passed_along(x, axis, by):
    length = lax.axis_size(axis)
    return lax.ppermute(x, axis, [(i, (i + by) % length) for i in range(length)])


def masked_attention(queries, keys_in, values, usable):
    factor = 1.0 / math.sqrt(queries.shape[-1])
    scores = (
        jnp.einsum("...ihe,...jhe->...hij", queries, keys_in, preferred_element_type=jnp.float32)
        * factor
    )
    allowed = usable[..., None, :, None] & usable[..., None, None, :]
    masked = jnp.where(allowed, scores, NEG_FILL)
    highest = jnp.max(masked, axis=-1, keepdims=True)
    raised = jnp.where(allowed, jnp.exp(masked - highest), 0.0)
    spare_one = jnp.where(usable, 0.0, 1.0)[..., None, :, None]
    weights = (raised / (jnp.sum(raised, axis=-1, keepdims=True) + spare_one)).astype(jnp.bfloat16)
    blended = jnp.einsum(
        "...hij,...jhe->...ihe", weights, values, preferred_element_type=jnp.float32
    )
    return blended.astype(jnp.bfloat16)


SEQ = ("zh", "x", "c")


def seq_index():
    return (lax.axis_index("zh") * lax.axis_size("x") + lax.axis_index("x")) * lax.axis_size(
        "c"
    ) + lax.axis_index("c")


def gather_seq(block):
    across = lax.all_gather(block, "zh", axis=0)
    along = lax.all_gather(across, "x", axis=1)
    both = lax.all_gather(along, "c", axis=2)
    return both.reshape((-1,) + block.shape[1:])


def relay_features(rows_now):
    return lax.all_to_all(rows_now, SEQ, split_axis=0, concat_axis=0, tiled=True)


def pass_onward(rows_now):
    return passed_along(rows_now, "segment", 1)


def on_device(latents, w_qkv, w_out, mod_shift, mod_scale, mod_gate, counts):
    frames = lax.axis_size(SEQ)
    patches = latents.shape[2]
    narrow = latents.shape[3]
    span = patches // frames
    segment_rows = latents[0, 0]
    gathered = lax.all_gather(latents, "mp", axis=3, tiled=True)[0, 0]
    widened = gathered.astype(jnp.float32)
    average = jnp.mean(widened, axis=-1, keepdims=True)
    centred = widened - average
    variance = jnp.mean(centred * centred, axis=-1, keepdims=True)
    modulated = (centred * lax.rsqrt(variance + EPS) * mod_scale[0] + mod_shift[0]).astype(
        jnp.bfloat16
    )
    columns = w_qkv.shape[2] * w_qkv.shape[3]
    piece = gather_seq(w_qkv[0])
    height = piece.shape[0]
    projected = jnp.dot(
        modulated, piece.reshape(height, columns), preferred_element_type=jnp.float32
    )
    local_heads = w_qkv.shape[3] // HD
    projected = projected.astype(jnp.bfloat16).reshape(patches, 3, local_heads, HD)
    frame_here = seq_index()
    clip_counts = counts[0]
    positions = jnp.arange(frames)

    def spatial(triple):
        count_here = jnp.sum(jnp.where(positions == frame_here, clip_counts, 0))
        usable = jnp.arange(patches) < count_here
        return masked_attention(triple[:, 0], triple[:, 1], triple[:, 2], usable)

    def temporal(triple):
        by_place = triple.reshape(frames, span, 3, local_heads, HD).transpose(1, 0, 2, 3, 4)
        location = frame_here * span + jnp.arange(span)
        usable = location[:, None] < clip_counts[None, :]
        blended = masked_attention(by_place[:, :, 0], by_place[:, :, 1], by_place[:, :, 2], usable)
        return blended.transpose(1, 0, 2, 3).reshape(patches, local_heads, HD)

    attended = lax.cond(lax.axis_index("segment") % 2 == 0, spatial, temporal, projected)
    attended = attended.reshape(patches, local_heads * HD)
    out_blocks = gather_seq(w_out[0][None])
    member = lax.axis_index("mp")
    partials = jnp.einsum(
        "tr,brc->tbc", attended, out_blocks, preferred_element_type=jnp.float32
    ).reshape(patches, -1)
    summed = lax.psum_scatter(
        partials.astype(jnp.bfloat16), "mp", scatter_dimension=1, tiled=True
    ).astype(jnp.float32)
    gate_here = lax.dynamic_slice_in_dim(mod_gate[0], member * narrow, narrow)
    updated = (segment_rows.astype(jnp.float32) + gate_here * summed).astype(jnp.bfloat16)
    updated = updated.reshape(frames, span, narrow)
    moved = pass_onward(relay_features(updated))
    return moved.reshape(1, 1, patches, narrow)


def solution(mesh):
    seg, seq, mp = mesh.devices.shape
    inner = mesh.devices.reshape(seg, 2, seq // 4, 2, mp)
    fine = jax.sharding.Mesh(inner, ("segment", "zh", "x", "c", "mp"))
    return jax.shard_map(
        on_device,
        mesh=fine,
        in_specs=(
            P("segment", SEQ, None, "mp"),
            P("segment", SEQ, None, "mp"),
            P("segment", "mp", SEQ),
            P("segment", None),
            P("segment", None),
            P("segment", None),
            P("segment", None),
        ),
        out_specs=P("segment", SEQ, None, "mp"),
        check_vma=False,
    )
```

profile of v0, /device:TPU:1, one launch (start us, length us, event | category | flops | bytes accessed | tf_op | source)
XLA Modules:
  0.0 409.4 jit_solution(5378004970461024760)
XLA Ops:
  6.5 0.7 all-gather.14.cloned.1.call-update
  7.3 19.6 %all-gather.2 = bf16[2,512,256]{2,1,0:T(8,128)(2,1)} all-gather(bf16[1,512,256]{2,1,0:T(8,128)(2,1)} %param.11), channel_id=4, replica_groups=mesh['segment'=4,'zh'=2,'x'=4,'c'=2,'mp'=8] {'zh'}, dimensions={0}, use_global_device_ids=true | all-gather | bytes 786432 | tf_op jit(solution)/shard_map/all_gather | solution.py:45
  26.9 0.0 all-gather.16.cloned.1.call-start
  26.9 44.4 %all-gather.14.cloned.1.call-done = bf16[2,256,3,512]{3,1,2,0:T(8,128)(2,1)} async-done(((bf16[1,256,3,512]{3,1,2,0:T(8,128)(2,1)}), bf16[2,256,3,512]{3,1,2,0:T(8,128)(2,1)}) %all-gather.14.cloned.1.call-update) | async-done | bytes 1572880 | tf_op jit(solution)/shard_map/all_gather | solution.py:45
  71.4 0.5 all-gather.12.cloned.1.call-update
  72.0 34.1 %all-gather.20.cloned.1.call-done = bf16[2,2048,256]{2,1,0:T(8,128)(2,1)} async-done(((bf16[2,512,256]{2,1,0:T(8,128)(2,1)}), bf16[2,2048,256]{2,1,0:T(8,128)(2,1)}) %all-gather.20.cloned.1.call-update) | async-done | bytes 2097168 | tf_op jit(solution)/shard_map/all_gather | solution.py:46
  106.2 73.1 %all-gather.16.cloned.1.call-done = bf16[2,1024,3,512]{3,1,2,0:T(8,128)(2,1)} async-done(((bf16[2,256,3,512]{3,1,2,0:T(8,128)(2,1)}), bf16[2,1024,3,512]{3,1,2,0:T(8,128)(2,1)}) %all-gather.16.cloned.1.call-update) | async-done | bytes 6291472 | tf_op jit(solution)/shard_map/all_gather | solution.py:46
  179.3 11.4 %copy.28 = bf16[2,4,256,3,512]{2,1,0,4,3:T(4,128)(2,1)} copy(bf16[2,4,256,3,512]{4,2,1,3,0:T(8,128)(2,1)} %bitcast.90) | data formatting | bytes 12582912 | tf_op jit(solution)/shard_map/all_gather | solution.py:46
  190.8 0.0 reduce-scatter.2.cloned.1.call-start
  190.8 30.5 %all-gather.12.cloned.1.call-done = bf16[1,1,256,4096]{3,2,1,0:T(8,128)(2,1)} async-done(((bf16[1,1,256,512]{3,2,1,0:T(8,128)(2,1)}), bf16[1,1,256,4096]{3,2,1,0:T(8,128)(2,1)}) %all-gather.12.cloned.1.call-update) | async-done | bytes 2097168 | tf_op jit(solution)/shard_map/all_gather | solution.py:65
  221.4 2.0 convert_reduce_fusion
  223.3 2.3 fusion.30
  225.6 23.9 %all-gather.22.cloned.1.call-done = bf16[2,4,2,512,256]{4,3,2,1,0:T(8,128)(2,1)} async-done(((bf16[2,4,1,512,256]{4,3,2,1,0:T(8,128)(2,1)}), bf16[2,4,2,512,256]{4,3,2,1,0:T(8,128)(2,1)}) %all-gather.22.cloned.1.call-update) | async-done | bytes 4194320 | tf_op jit(solution)/shard_map/all_gather | solution.py:47
  249.5 6.4 %copy.30 = bf16[16,256,512]{2,1,0:T(8,128)(2,1)} copy(bf16[16,256,512]{1,2,0:T(8,128)(2,1)} %bitcast.91) | data formatting | bytes 8388608 | tf_op jit(solution)/shard_map/tr,brc->tbc/dot_general | solution.py:101
  255.9 29.7 %all-gather.18.cloned.1.call-done = bf16[2,4,512,3,512]{2,1,0,4,3:T(4,128)(2,1)} async-done(((bf16[2,4,256,3,512]{2,1,0,4,3:T(4,128)(2,1)}), bf16[2,4,512,3,512]{2,1,0,4,3:T(4,128)(2,1)}) %all-gather.18.cloned.1.call-update) | async-done | bytes 12582928 | tf_op jit(solution)/shard_map/all_gather | solution.py:47
  285.6 21.0 %reshape_reshape.6 = bf16[4096,1536]{0,1:T(8,128)(2,1)} reshape(bf16[2,4,512,3,512]{2,1,0,4,3:T(4,128)(2,1)} %all-gather.18.cloned.1.call-done) | data formatting | bytes 25165824 | tf_op jit(solution)/shard_map/reshape;reshape | solution.py:77
  306.6 8.1 %convolution_convert_fusion.3 = bf16[256,1536]{1,0:T(8,128)(2,1)S(1)} fusion(bf16[4096,1536]{0,1:T(8,128)(2,1)} %reshape_reshape.6, bf16[1,1,256,4096]{3,2,1,0:T(8,128)(2,1)S(1)} %copy-done.1, f32[4096]{0:T(1024)S(1)} %bitcast.105, f32[4096]{0:T(1024)S(1)} %bitcast.106, f32[256]{0:T(256)S(1)} %add_rsqrt_fusion, f32[256]{0:T(256)S(1)} %broadcast_multiply_fusion), kind=kOutput, calls=%fused_computation.57 | convolution fusion | flops 3227910144 | bytes 15501312 | tf_op jit(solution)/shard_map/dot_general | solution.py:76
  314.7 4.0 conditional.1
  314.8 0.7 fusion.14
  315.5 0.3 copy.29
  315.7 0.7 iota_compare_fusion
  316.4 0.7 broadcast_select_fusion.1
  317.1 0.1 broadcast_and_fusion.1
  317.2 0.6 fusion.39
  317.9 0.8 convolution_convert_fusion.1
  318.7 4.9 %convolution_convert_fusion.2 = bf16[256,4096]{1,0:T(8,128)(2,1)} fusion(bf16[256,512]{0,1:T(8,128)(2,1)S(1)} %get-tuple-element.40, bf16[4096,512]{1,0:T(8,128)(2,1)} %bitcast.89), kind=kOutput, calls=%fused_computation.49 | convolution fusion | flops 1074790400 | bytes 6553600 | tf_op jit(solution)/shard_map/tr,brc->tbc/dot_general | solution.py:101
  323.7 40.9 %reduce-scatter.2.cloned.1.call-done = bf16[256,512]{1,0:T(8,128)(2,1)} async-done(((bf16[256,4096]{1,0:T(8,128)(2,1)}), bf16[256,512]{1,0:T(8,128)(2,1)}) %reduce-scatter.2.cloned.1.call-update) | async-done | bytes 262160 | tf_op jit(solution)/shard_map/reduce_scatter | solution.py:104
  364.5 1.0 fusion.37
  365.6 25.7 %all_to_all.5 = bf16[16,16,512]{2,1,0:T(8,128)(2,1)S(1)} all-to-all(bf16[16,16,512]{2,1,0:T(8,128)(2,1)S(1)} %bitcast.93), channel_id=1, replica_groups=mesh['segment'=4,'zh'=2,'x'=4,'c'=2,'mp'=8] {'zh','x','c'}, dimensions={0} | all-to-all | bytes 524288 | tf_op jit(solution)/shard_map/all_to_all | solution.py:52
  391.2 4.9 %collective-permute-start = (bf16[16,16,512]{2,1,0:T(8,128)(2,1)S(1)}, bf16[16,16,512]{2,1,0:T(8,128)(2,1)S(1)}, u32[]{:S(2)}, u32[]{:S(2)}) collective-permute-start(bf16[16,16,512]{2,1,0:T(8,128)(2,1)S(1)} %all_to_all.5), channel_id=1, source_target_pairs={{0,128},{128,256},{256,384},{384,0},{1,129},{129,257},{257,385},{3... | collective-permute-start | bytes 786440 | tf_op jit(solution)/shard_map/ppermute | solution.py:14
  396.2 5.6 %collective-permute-done = bf16[16,16,512]{2,1,0:T(8,128)(2,1)S(1)} collective-permute-done((bf16[16,16,512]{2,1,0:T(8,128)(2,1)S(1)}, bf16[16,16,512]{2,1,0:T(8,128)(2,1)S(1)}, u32[]{:S(2)}, u32[]{:S(2)}) %collective-permute-start) | collective-permute-done | bytes 262176 | tf_op jit(solution)/shard_map/ppermute | solution.py:14
  401.8 0.7 copy.43
  (27 shorter events, 0.3 us)
Async XLA Ops:
  6.5 317.1 %copy-start = (f32[1,4096]{1,0:T(1,128)S(1)}, f32[1,4096]{1,0:T(1,128)}, u32[]{:S(2)}) copy-start(f32[1,4096]{1,0:T(1,128)} %param.14) | copy-start | bytes 49156
  6.5 64.8 %all-gather.14.cloned.1.call-start = ((), (), s32[]{:S(2)}) async-start(), calls=%async_computation.3 | async-start | bytes 2359296 | tf_op jit(solution)/shard_map/all_gather | solution.py:45
  7.3 98.9 %all-gather.20.cloned.1.call-start = ((), (), s32[]{:S(2)}) async-start(), calls=%async_computation.7 | async-start | bytes 2621440 | tf_op jit(solution)/shard_map/all_gather | solution.py:46
  26.9 152.4 %all-gather.16.cloned.1.call-start = ((), (), s32[]{:S(2)}) async-start(), calls=%async_computation.5 | async-start | bytes 7864320 | tf_op jit(solution)/shard_map/all_gather | solution.py:46
  71.4 150.0 %all-gather.12.cloned.1.call-start = ((), (), s32[]{:S(2)}) async-start(), calls=%async_computation.2 | async-start | bytes 2359296 | tf_op jit(solution)/shard_map/all_gather | solution.py:65
  72.0 177.5 %all-gather.22.cloned.1.call-start = ((), (), s32[]{:S(2)}) async-start(), calls=%async_computation.8 | async-start | bytes 6291456 | tf_op jit(solution)/shard_map/all_gather | solution.py:47
  106.2 179.4 %all-gather.18.cloned.1.call-start = ((), (), s32[]{:S(2)}) async-start(), calls=%async_computation.6 | async-start | bytes 18874368 | tf_op jit(solution)/shard_map/all_gather | solution.py:47
  190.8 173.8 %reduce-scatter.2.cloned.1.call-start = ((), (), s32[]{:S(2)}) async-start(), calls=%async_computation.4 | async-start | bytes 2359296 | tf_op jit(solution)/shard_map/reduce_scatter | solution.py:104
  255.9 50.7 %copy-start.1 = (bf16[1,1,256,4096]{3,2,1,0:T(8,128)(2,1)S(1)}, bf16[1,1,256,4096]{3,2,1,0:T(8,128)(2,1)}, u32[]{:S(2)}) copy-start(bf16[1,1,256,4096]{3,2,1,0:T(8,128)(2,1)} %all-gather.12.cloned.1.call-done) | copy-start | bytes 6291460
  255.9 50.7 %copy-start.4 = (f32[1,4096]{1,0:T(1,128)S(1)}, f32[1,4096]{1,0:T(1,128)}, u32[]{:S(2)}) copy-start(f32[1,4096]{1,0:T(1,128)} %param.12) | copy-start | bytes 49156
  255.9 50.7 %copy-start.5 = (f32[1,4096]{1,0:T(1,128)S(1)}, f32[1,4096]{1,0:T(1,128)}, u32[]{:S(2)}) copy-start(f32[1,4096]{1,0:T(1,128)} %param.13) | copy-start | bytes 49156
  306.6 8.1 %copy-start.3 = (s32[1,16]{1,0:T(1,128)S(1)}, s32[1,16]{1,0:T(1,128)}, u32[]{:S(2)}) copy-start(s32[1,16]{1,0:T(1,128)} %param.15) | copy-start | bytes 196
  318.7 45.8 %copy-start.2 = (bf16[1,1,256,512]{3,2,1,0:T(8,128)(2,1)S(1)}, bf16[1,1,256,512]{3,2,1,0:T(8,128)(2,1)}, u32[]{:S(2)}) copy-start(bf16[1,1,256,512]{3,2,1,0:T(8,128)(2,1)} %param.9) | copy-start | bytes 786436
  391.2 10.6 %collective-permute-start = (bf16[16,16,512]{2,1,0:T(8,128)(2,1)S(1)}, bf16[16,16,512]{2,1,0:T(8,128)(2,1)S(1)}, u32[]{:S(2)}, u32[]{:S(2)}) collective-permute-start(bf16[16,16,512]{2,1,0:T(8,128)(2,1)S(1)} %all_to_all.5), channel_id=1, source_target_pairs={{0,128},{128,256},{256,384},{384,0},{1,129},{129,257},{257,385},{3... | collective-permute-start | bytes 786440 | tf_op jit(solution)/shard_map/ppermute | solution.py:14
Sparse Core Ops, SparseCore 0:
  9.4 61.9 all-gather.13
  73.5 32.6 all-gather.19
  108.2 71.0 all-gather.15
  181.3 40.0 all-gather.11
  223.3 26.1 all-gather.21
  251.5 34.0 all-gather.17
  323.8 40.7 reduce-scatter.1
where the time goes:
time: 411 us; the launch traced here: 409 us
  waiting for transfers between devices  284 us (69%)
  blocking collectives  45.2 us (11%)
  local copies, waits for them, and re-layouts  39.8 us (10%)
  matrix products  14.4 us (4%)
  between operations  13.6 us (3%)
  other arithmetic  7.48 us (2%)
  starting transfers between devices  5.16 us (1%)
    all_gather x2, waiting for transfers between devices, gather_seq(): along = lax.all_gather(across, 'x', axis=1)  107 us
    all_gather x2, waiting for transfers between devices, gather_seq(): both = lax.all_gather(along, 'c', axis=2)  53.6 us
    all_gather x1, waiting for transfers between devices, gather_seq(): across = lax.all_gather(block, 'zh', axis=0)  44.4 us
    reduce_scatter x1, waiting for transfers between devices, on_device(): lax.psum_scatter(partials.astype(jnp.bfloat16), 'mp', scatter_dimension=1...  40.9 us
    all_gather x1, waiting for transfers between devices, on_device(): gathered = lax.all_gather(latents, 'mp', axis=3, tiled=True)[0, 0]  30.5 us
    all_to_all x1, blocking collectives, relay_features(): lax.all_to_all(rows_now, SEQ, split_axis=0, concat_axis=0, tiled=True)  25.7 us
    another operation x1, local copies, waits for them, and re-layouts, on_device(): piece.reshape(height, columns)  21 us
    all_gather x1, blocking collectives, gather_seq(): across = lax.all_gather(block, 'zh', axis=0)  19.6 us
  transfers between devices with their start and end apart: 8, of which 8 were waited for; matrix products, arithmetic and copies ran while one was open for 5% of the time, Pallas kernels for 0%

commit v1 on v0

--- a/solution.py
+++ b/solution.py
@@ -3,6 +3,7 @@
 import jax.numpy as jnp
 from jax import lax
 from jax.sharding import PartitionSpec as P
+from jax.lax import all_to_all, axis_size
 
 HD = 128
 EPS = 1e-06
@@ -62,7 +63,9 @@
     narrow = latents.shape[3]
     span = patches // frames
     segment_rows = latents[0, 0]
-    gathered = lax.all_gather(latents, "mp", axis=3, tiled=True)[0, 0]
+    gathered = jnp.concatenate(
+        all_to_all(jnp.stack([latents for _ in range(axis_size("mp"))], axis=0), "mp", 0, 0), axis=3
+    )[0, 0]
     widened = gathered.astype(jnp.float32)
     average = jnp.mean(widened, axis=-1, keepdims=True)
     centred = widened - average

time: 411 us -> 381 us (0.927)
  waiting for transfers between devices: 284 us -> 245 us
  starting transfers between devices: 5.16 us -> 11.8 us
    all_gather x2, waiting for transfers between devices: 53.6 us -> 0.01 us  [gather_seq(): both = lax.all_gather(along, 'c', axis=2)]
    all_to_all x0 -> x1, waiting for transfers between devices: none -> 49.9 us  [on_device(): all_to_all(jnp.stack([latents for _ in range(axis_size('mp'))], axis=0),...]
    all_gather x1 -> x0, waiting for transfers between devices: 30.5 us -> none  [on_device(): gathered = lax.all_gather(latents, 'mp', axis=3, tiled=True)[0, 0]]
    all_to_all x0 -> x1, starting transfers between devices: none -> 6.46 us  [on_device(): all_to_all(jnp.stack([latents for _ in range(axis_size('mp'))], axis=0),...]
    reduce_scatter x1, waiting for transfers between devices: 40.9 us -> 36.3 us  [on_device(): lax.psum_scatter(partials.astype(jnp.bfloat16), 'mp', scatter_dimension=1...]
  transfers between devices with their start and end apart: 8 -> 8, of which waited for: 8 -> 6; matrix products, arithmetic and copies ran while one was open for 5% -> 7% of each run, Pallas kernels for 0% -> 0%
where the time goes in v1:
time: 381 us; the launch traced here: 380 us
  waiting for transfers between devices  245 us (64%)
  blocking collectives  45.5 us (12%)
  local copies, waits for them, and re-layouts  43 us (11%)
  between operations  13.6 us (4%)
  matrix products  12.9 us (3%)
  starting transfers between devices  11.8 us (3%)
  other arithmetic  8.2 us (2%)
    all_gather x2, waiting for transfers between devices, gather_seq(): along = lax.all_gather(across, 'x', axis=1)  108 us
    all_to_all x1, waiting for transfers between devices, on_device(): all_to_all(jnp.stack([latents for _ in range(axis_size('mp'))], axis=0),...  49.9 us
    all_gather x1, waiting for transfers between devices, gather_seq(): across = lax.all_gather(block, 'zh', axis=0)  44.4 us
    reduce_scatter x1, waiting for transfers between devices, on_device(): lax.psum_scatter(partials.astype(jnp.bfloat16), 'mp', scatter_dimension=1...  36.3 us
    all_to_all x1, blocking collectives, relay_features(): lax.all_to_all(rows_now, SEQ, split_axis=0, concat_axis=0, tiled=True)  26 us
    another operation x1, local copies, waits for them, and re-layouts, on_device(): piece.reshape(height, columns)  21.1 us
    all_gather x1, blocking collectives, gather_seq(): across = lax.all_gather(block, 'zh', axis=0)  19.6 us
    all_gather x1, local copies, waits for them, and re-layouts, gather_seq(): along = lax.all_gather(across, 'x', axis=1)  11.4 us
  transfers between devices with their start and end apart: 8, of which 6 were waited for; matrix products, arithmetic and copies ran while one was open for 7% of the time, Pallas kernels for 0%

profile of v1, /device:TPU:1, one launch (start us, length us, event | category | flops | bytes accessed | tf_op | source)
XLA Modules:
  0.0 379.8 jit_solution(12474662875677199753)
XLA Ops:
  6.5 0.7 all-gather.11.cloned.1.call-update
  7.3 19.6 %all-gather.2 = bf16[2,512,256]{2,1,0:T(8,128)(2,1)} all-gather(bf16[1,512,256]{2,1,0:T(8,128)(2,1)} %param.11), channel_id=4, replica_groups=mesh['segment'=4,'zh'=2,'x'=4,'c'=2,'mp'=8] {'zh'}, dimensions={0}, use_global_device_ids=true | all-gather | bytes 786432 | tf_op jit(solution)/shard_map/all_gather | solution.py:46
  26.9 44.4 %all-gather.11.cloned.1.call-done = bf16[2,256,3,512]{3,1,2,0:T(8,128)(2,1)} async-done(((bf16[1,256,3,512]{3,1,2,0:T(8,128)(2,1)}), bf16[2,256,3,512]{3,1,2,0:T(8,128)(2,1)}) %all-gather.11.cloned.1.call-update) | async-done | bytes 1572880 | tf_op jit(solution)/shard_map/all_gather | solution.py:46
  71.4 34.7 %all-gather.17.cloned.1.call-done = bf16[2,2048,256]{2,1,0:T(8,128)(2,1)} async-done(((bf16[2,512,256]{2,1,0:T(8,128)(2,1)}), bf16[2,2048,256]{2,1,0:T(8,128)(2,1)}) %all-gather.17.cloned.1.call-update) | async-done | bytes 2097168 | tf_op jit(solution)/shard_map/all_gather | solution.py:47
  106.2 73.1 %all-gather.13.cloned.1.call-done = bf16[2,1024,3,512]{3,1,2,0:T(8,128)(2,1)} async-done(((bf16[2,256,3,512]{3,1,2,0:T(8,128)(2,1)}), bf16[2,1024,3,512]{3,1,2,0:T(8,128)(2,1)}) %all-gather.13.cloned.1.call-update) | async-done | bytes 6291472 | tf_op jit(solution)/shard_map/all_gather | solution.py:47
  179.3 11.4 %copy.31 = bf16[2,4,256,3,512]{2,1,0,4,3:T(4,128)(2,1)} copy(bf16[2,4,256,3,512]{4,2,1,3,0:T(8,128)(2,1)} %bitcast.84) | data formatting | bytes 12582912 | tf_op jit(solution)/shard_map/all_gather | solution.py:47
  190.8 0.9 copy-done.2
  191.8 1.5 stack.2
  193.4 6.5 %all-to-all-start = ((bf16[8,1,1,256,512]{3,4,2,1,0:T(8,128)(2,1)}), bf16[8,1,1,256,512]{3,4,2,1,0:T(8,128)(2,1)S(1)}, u32[]{:S(2)}, u32[]{:S(2)}) async-start(bf16[8,1,1,256,512]{3,4,2,1,0:T(8,128)(2,1)} %stack.2), calls=%async_computation | async-start | bytes 4194304 | tf_op jit(solution)/shard_map/all_to_all | solution.py:67
  199.9 0.5 broadcast.210
  200.4 0.6 reduce.10
  201.0 0.6 reduce.11
  201.6 49.9 %all-to-all-done = bf16[8,1,1,256,512]{3,4,2,1,0:T(8,128)(2,1)S(1)} async-done(((bf16[8,1,1,256,512]{3,4,2,1,0:T(8,128)(2,1)}), bf16[8,1,1,256,512]{3,4,2,1,0:T(8,128)(2,1)S(1)}, u32[]{:S(2)}, u32[]{:S(2)}) %all-to-all-start) | async-done | bytes 2097184 | tf_op jit(solution)/shard_map/all_to_all | solution.py:67
  251.5 0.6 convert_reduce_fusion
  252.1 0.6 fusion.26
  252.7 2.7 fusion.29
  255.3 6.4 %copy.33 = bf16[16,256,512]{2,1,0:T(8,128)(2,1)} copy(bf16[16,256,512]{1,2,0:T(8,128)(2,1)} %bitcast.85) | data formatting | bytes 8388608 | tf_op jit(solution)/shard_map/tr,brc->tbc/dot_general | solution.py:104
  261.7 21.1 %reshape_reshape.6 = bf16[4096,1536]{0,1:T(8,128)(2,1)} reshape(bf16[2,4,512,3,512]{2,1,0,4,3:T(4,128)(2,1)} %all-gather.15.cloned.1.call-done) | data formatting | bytes 25165824 | tf_op jit(solution)/shard_map/reshape;reshape | solution.py:80
  282.9 6.6 %convolution_convert_fusion.3 = bf16[256,1536]{1,0:T(8,128)(2,1)S(1)} fusion(bf16[256,4096]{0,1:T(8,128)(2,1)S(1)} %bitcast.87, bf16[4096,1536]{0,1:T(8,128)(2,1)} %reshape_reshape.6), kind=kOutput, calls=%fused_computation.55 | convolution fusion | flops 3221618688 | bytes 15466496 | tf_op jit(solution)/shard_map/dot_general | solution.py:79
  289.5 4.0 %conditional.1 = (bf16[256,512]{0,1:T(8,128)(2,1)S(1)}) conditional(s32[]{:T(128)} %convert_element_type.51, (s32[]{:T(128)}, s32[1,16]{1,0:T(1,128)S(1)}, bf16[256,1536]{1,0:T(8,128)(2,1)S(1)}) %tuple.31, (s32[]{:T(128)}, s32[16]{0:T(128)S(1)}, s32[1,16]{1,0:T(1,128)S(1)}, bf16[256,1536]{1,0:T(8,128)(2,1)S(1)}) %tuple.32), branch_computations={%region_2.5_spmd, %region_5.9_spmd} | conditional | flops 204410160 | bytes 6552408 | solution.py:100
  289.5 0.7 fusion.14
  290.5 0.7 iota_compare_fusion
  291.2 0.7 broadcast_select_fusion.1
  292.0 0.6 fusion.31
  292.6 0.8 convolution_convert_fusion.1
  293.5 4.9 %convolution_convert_fusion.2 = bf16[256,4096]{1,0:T(8,128)(2,1)} fusion(bf16[256,512]{0,1:T(8,128)(2,1)S(1)} %get-tuple-element.40, bf16[4096,512]{1,0:T(8,128)(2,1)} %bitcast.83), kind=kOutput, calls=%fused_computation.48 | convolution fusion | flops 1074790400 | bytes 6553600 | tf_op jit(solution)/shard_map/tr,brc->tbc/dot_general | solution.py:104
  298.4 36.3 %reduce-scatter.2.cloned.1.call-done = bf16[256,512]{1,0:T(8,128)(2,1)} async-done(((bf16[256,4096]{1,0:T(8,128)(2,1)}), bf16[256,512]{1,0:T(8,128)(2,1)}) %reduce-scatter.2.cloned.1.call-update) | async-done | bytes 262160 | tf_op jit(solution)/shard_map/reduce_scatter | solution.py:107
  334.7 1.0 add_convert_fusion
  335.7 26.0 %all_to_all.10 = bf16[16,16,512]{2,1,0:T(8,128)(2,1)S(1)} all-to-all(bf16[16,16,512]{2,1,0:T(8,128)(2,1)S(1)} %bitcast.89), channel_id=1, replica_groups=mesh['segment'=4,'zh'=2,'x'=4,'c'=2,'mp'=8] {'zh','x','c'}, dimensions={0} | all-to-all | bytes 524288 | tf_op jit(solution)/shard_map/all_to_all | solution.py:53
  361.7 5.1 %collective-permute-start = (bf16[16,16,512]{2,1,0:T(8,128)(2,1)S(1)}, bf16[16,16,512]{2,1,0:T(8,128)(2,1)S(1)}, u32[]{:S(2)}, u32[]{:S(2)}) collective-permute-start(bf16[16,16,512]{2,1,0:T(8,128)(2,1)S(1)} %all_to_all.10), channel_id=1, source_target_pairs={{0,128},{128,256},{256,384},{384,0},{1,129},{129,257},{257,385},{3... | collective-permute-start | bytes 786440 | tf_op jit(solution)/shard_map/ppermute | solution.py:15
  366.8 5.4 %collective-permute-done = bf16[16,16,512]{2,1,0:T(8,128)(2,1)S(1)} collective-permute-done((bf16[16,16,512]{2,1,0:T(8,128)(2,1)S(1)}, bf16[16,16,512]{2,1,0:T(8,128)(2,1)S(1)}, u32[]{:S(2)}, u32[]{:S(2)}) %collective-permute-start) | collective-permute-done | bytes 262176 | tf_op jit(solution)/shard_map/ppermute | solution.py:15
  372.2 0.7 copy.46
  (34 shorter events, 0.8 us)
Async XLA Ops:
  6.5 291.8 %copy-start = (f32[1,4096]{1,0:T(1,128)S(1)}, f32[1,4096]{1,0:T(1,128)}, u32[]{:S(2)}) copy-start(f32[1,4096]{1,0:T(1,128)} %param.14) | copy-start | bytes 49156
  6.5 64.8 %all-gather.11.cloned.1.call-start = ((), (), s32[]{:S(2)}) async-start(), calls=%async_computation.3 | async-start | bytes 2359296 | tf_op jit(solution)/shard_map/all_gather | solution.py:46
  7.3 98.9 %all-gather.17.cloned.1.call-start = ((), (), s32[]{:S(2)}) async-start(), calls=%async_computation.7 | async-start | bytes 2621440 | tf_op jit(solution)/shard_map/all_gather | solution.py:47
  26.9 152.4 %all-gather.13.cloned.1.call-start = ((), (), s32[]{:S(2)}) async-start(), calls=%async_computation.5 | async-start | bytes 7864320 | tf_op jit(solution)/shard_map/all_gather | solution.py:47
  71.4 183.9 %all-gather.19.cloned.1.call-start = ((), (), s32[]{:S(2)}) async-start(), calls=%async_computation.8 | async-start | bytes 6291456 | tf_op jit(solution)/shard_map/all_gather | solution.py:48
  106.2 155.6 %all-gather.15.cloned.1.call-start = ((), (), s32[]{:S(2)}) async-start(), calls=%async_computation.6 | async-start | bytes 18874368 | tf_op jit(solution)/shard_map/all_gather | solution.py:48
  190.8 0.9 copy-start.2
  190.8 9.6 %copy-start.3 = (f32[1,4096]{1,0:T(1,128)S(1)}, f32[1,4096]{1,0:T(1,128)}, u32[]{:S(2)}) copy-start(f32[1,4096]{1,0:T(1,128)} %param.12) | copy-start | bytes 49156
  190.8 10.2 %copy-start.4 = (f32[1,4096]{1,0:T(1,128)S(1)}, f32[1,4096]{1,0:T(1,128)}, u32[]{:S(2)}) copy-start(f32[1,4096]{1,0:T(1,128)} %param.13) | copy-start | bytes 49156
  193.4 58.1 %all-to-all-start = ((bf16[8,1,1,256,512]{3,4,2,1,0:T(8,128)(2,1)}), bf16[8,1,1,256,512]{3,4,2,1,0:T(8,128)(2,1)S(1)}, u32[]{:S(2)}, u32[]{:S(2)}) async-start(bf16[8,1,1,256,512]{3,4,2,1,0:T(8,128)(2,1)} %stack.2), calls=%async_computation | async-start | bytes 4194304 | tf_op jit(solution)/shard_map/all_to_all | solution.py:67
  199.8 134.8 %reduce-scatter.2.cloned.1.call-start = ((), (), s32[]{:S(2)}) async-start(), calls=%async_computation.4 | async-start | bytes 2359296 | tf_op jit(solution)/shard_map/reduce_scatter | solution.py:107
  261.7 21.1 %copy-start.1 = (bf16[8,1,1,256,512]{3,4,0,2,1:T(8,128)(2,1)S(1)}, bf16[8,1,1,256,512]{3,4,0,2,1:T(8,128)(2,1)}, u32[]{:S(2)}) copy-start(bf16[8,1,1,256,512]{3,4,0,2,1:T(8,128)(2,1)} %fusion.29) | copy-start | bytes 6291460
  282.9 6.6 %copy-start.5 = (s32[1,16]{1,0:T(1,128)S(1)}, s32[1,16]{1,0:T(1,128)}, u32[]{:S(2)}) copy-start(s32[1,16]{1,0:T(1,128)} %param.15) | copy-start | bytes 196
  361.7 10.6 %collective-permute-start = (bf16[16,16,512]{2,1,0:T(8,128)(2,1)S(1)}, bf16[16,16,512]{2,1,0:T(8,128)(2,1)S(1)}, u32[]{:S(2)}, u32[]{:S(2)}) collective-permute-start(bf16[16,16,512]{2,1,0:T(8,128)(2,1)S(1)} %all_to_all.10), channel_id=1, source_target_pairs={{0,128},{128,256},{256,384},{384,0},{1,129},{129,257},{257,385},{3... | collective-permute-start | bytes 786440 | tf_op jit(solution)/shard_map/ppermute | solution.py:15
Sparse Core Ops, SparseCore 0:
  9.4 61.9 all-gather.10
  73.5 32.6 all-gather.16
  108.2 71.0 all-gather.12
  181.3 24.1 all-gather.18
  207.4 34.0 all-gather.14
  298.5 36.1 reduce-scatter.1
